TPU v7x, 256 devices: a whole 4x4x8 slice. The times are simulated.
256 devices in a mesh: req: 32 (over x, z), tp: 8 (over y, core).
Axes of the slice: x: 4, y: 4, z: 8, core: 2. Of those that a mesh axis runs over, the one named last changes fastest.
Arguments:
- hidden: bfloat16 [4096, 2048], P('req', 'tp'), may hold values from -3 to 3
- lengths: int32 [4096], P('req'), may hold values from 1 to 1921, as said below
- routes: int32 [4096, 6], P('req'), may hold values from 0 to 63, all different within a row; in each aligned block of 128 rows (0 to 127, 128 to 255, ...) at most 32 rows name the same one
- latent_cache: bfloat16 [65536, 576], P('req'), may hold values from -400 to 400
- attention_gain: bfloat16 [2048], replicated, may hold values from 0.099609375 to 1.8984375
- query_weight: bfloat16 [2048, 3072], P(None, 'tp'), may hold values from -0.125 to 0.125
- latent_weight: bfloat16 [2048, 576], P(None, 'tp'), may hold values from -0.125 to 0.125
- latent_gain: bfloat16 [512], replicated, may hold values from 0.099609375 to 1.8984375
- key_absorb: bfloat16 [16, 128, 512], P('tp'), may hold values from -0.5 to 0.5
- value_absorb: bfloat16 [16, 512, 128], P('tp'), may hold values from -0.5 to 0.5
- output_weight: bfloat16 [2048, 2048], P('tp'), may hold values from -0.75 to 0.75
- feedforward_gain: bfloat16 [2048], replicated, may hold values from 0.099609375 to 1.8984375
- router_weight: bfloat16 [2048, 64], replicated, may hold values from -0.0625 to 0.0625
- expert_gate: bfloat16 [64, 2048, 1408], P('req', None, 'tp'), may hold values from -0.25 to 0.25
- expert_up: bfloat16 [64, 2048, 1408], P('req', None, 'tp'), may hold values from -0.25 to 0.25
- expert_down: bfloat16 [64, 1408, 2048], P('req', 'tp'), may hold values from -0.4375 to 0.4375
- shared_gate: bfloat16 [2048, 1408], P(None, 'tp'), may hold values from -0.25 to 0.25
- shared_up: bfloat16 [2048, 1408], P(None, 'tp'), may hold values from -0.25 to 0.25
- shared_down: bfloat16 [1408, 2048], P('tp'), may hold values from -0.21875 to 0.21875
Outputs:
- next_hidden: bfloat16 [4096, 2048], P('req', 'tp')
- new_rows: bfloat16 [4096, 576], P('req')
Inputs may be any that keep to these rules, and one draw needn't show every extreme that they name: The lengths of the 128 requests of one index of req (aligned blocks of 128) sum to at most 2048, and to exactly 2048 on some index, where one request holds 1921. `routes`: among the rows of one index of req, no expert is named by more than 32 rows, a bound that some block reaches.
All inputs are finite; a program needn't handle non-finite values.
Results may differ from a plain program's by a relative error of at most 0.023.
The roundings to bfloat16 on the way count: a program that leaves them out, or rounds other values in their place, can miss the bound.
Values may be sent and summed in bfloat16 or wider, within the bound.
No kernel may reach another device: no remote copies, remote signals or barrier semaphores. Data moves between devices by JAX's collectives and lax.ppermute only.
A program may use at most 128 MiB of HBM per device.

v0:
```python
import jax
import jax.numpy as jnp
from jax import lax
from jax.sharding import PartitionSpec as P

rope_base = 50000.0
route_scale = 2.446
norm_eps = 1e-06


def rms_norm(values, gains):
    widened = values.astype(jnp.float32)
    factor = lax.rsqrt(jnp.mean(widened * widened, axis=-1, keepdims=True) + norm_eps)
    return widened * factor * gains.astype(jnp.float32)


def rotate(values, positions):
    half_width = values.shape[-1] // 2
    exponent = jnp.arange(half_width, dtype=jnp.float32) * (2.0 / values.shape[-1])
    angles = positions[..., None] * jnp.power(rope_base, -exponent)
    cosine = jnp.cos(angles)
    sine_part = jnp.sin(angles)
    first_half = values[..., :half_width]
    second_half = values[..., half_width:]
    return jnp.concatenate(
        [
            first_half * cosine - second_half * sine_part,
            first_half * sine_part + second_half * cosine,
        ],
        axis=-1,
    )


def attend(queries, cache_rows, lengths, new_rows, score_scale, latent_width):
    starts = jnp.cumsum(lengths) - lengths
    places = jnp.arange(cache_rows.shape[0], dtype=jnp.int32)
    inside = (places[None, :] >= starts[:, None]) & (places[None, :] < (starts + lengths)[:, None])
    scores = (
        jnp.einsum("rhk,jk->rhj", queries, cache_rows, preferred_element_type=jnp.float32)
        * score_scale
    )
    own_score = (
        jnp.einsum("rhk,rk->rh", queries, new_rows, preferred_element_type=jnp.float32)
        * score_scale
    )
    highest = jnp.maximum(
        jnp.max(jnp.where(inside[:, None, :], scores, -jnp.inf), axis=-1), own_score
    )
    weights = jnp.where(inside[:, None, :], jnp.exp(scores - highest[..., None]), 0.0)
    own_weight = jnp.exp(own_score - highest)
    totals = jnp.sum(weights, axis=-1) + own_weight
    probabilities = (weights / totals[..., None]).astype(jnp.bfloat16)
    own_prob = (own_weight / totals).astype(jnp.bfloat16)
    summed = jnp.einsum(
        "rhj,jl->rhl",
        probabilities,
        cache_rows[:, :latent_width],
        preferred_element_type=jnp.float32,
    )
    summed = summed + own_prob.astype(jnp.float32)[..., None] * new_rows[
        :, None, :latent_width
    ].astype(jnp.float32)
    return summed.astype(jnp.bfloat16)


def shards(
    hidden,
    lengths,
    routes,
    latent_cache,
    attention_gain,
    query_weight,
    latent_weight,
    latent_gain,
    key_absorb,
    value_absorb,
    output_weight,
    feedforward_gain,
    router_weight,
    expert_gate,
    expert_up,
    expert_down,
    shared_gate,
    shared_up,
    shared_down,
):
    token_count = hidden.shape[0]
    owner_count = lax.axis_size("req")
    column_width = hidden.shape[1]
    column_start = lax.axis_index("tp") * column_width
    heads_here = key_absorb.shape[0]
    nope_width = key_absorb.shape[1]
    latent_width = key_absorb.shape[2]
    whole = lax.all_gather(hidden, "tp", axis=1, tiled=True)
    normed = rms_norm(whole, attention_gain).astype(jnp.bfloat16)
    projected = jnp.dot(normed, query_weight, preferred_element_type=jnp.float32).reshape(
        token_count, heads_here, -1
    )
    rope_width = projected.shape[2] - nope_width
    positions = lengths.astype(jnp.float32)
    query_nope = projected[..., :nope_width].astype(jnp.bfloat16)
    query_rope = rotate(projected[..., nope_width:], positions[:, None]).astype(jnp.bfloat16)
    query_latent = jnp.einsum(
        "thn,hnl->thl", query_nope, key_absorb, preferred_element_type=jnp.float32
    ).astype(jnp.bfloat16)
    latent_part = jnp.dot(normed, latent_weight, preferred_element_type=jnp.float32).astype(
        jnp.bfloat16
    )
    latent_raw = lax.all_gather(latent_part, "tp", axis=1, tiled=True)
    latent_new = rms_norm(latent_raw[:, :latent_width], latent_gain)
    key_new = rotate(latent_raw[:, latent_width:].astype(jnp.float32), positions)
    new_rows = jnp.concatenate([latent_new, key_new], axis=-1).astype(jnp.bfloat16)
    queries = jnp.concatenate([query_latent, query_rope], axis=-1)
    attended = attend(
        queries, latent_cache, lengths, new_rows, (nope_width + rope_width) ** (-0.5), latent_width
    )
    head_values = jnp.einsum(
        "thl,hlv->thv", attended, value_absorb, preferred_element_type=jnp.float32
    ).astype(jnp.bfloat16)
    attention = jnp.dot(
        head_values.reshape(token_count, -1), output_weight, preferred_element_type=jnp.float32
    )
    total_attention = lax.psum(attention, "tp")
    mixed = (whole.astype(jnp.float32) + total_attention).astype(jnp.bfloat16)
    mixed_columns = lax.dynamic_slice_in_dim(mixed, column_start, column_width, 1)
    expert_in = rms_norm(mixed, feedforward_gain).astype(jnp.bfloat16)
    logits = jnp.dot(expert_in, router_weight, preferred_element_type=jnp.float32)
    expert_count = router_weight.shape[1]
    top_count = routes.shape[1]
    per_owner = expert_count // owner_count
    slot_count = max(2, 8 * token_count * top_count // (3 * expert_count))
    chosen = jnp.take_along_axis(jax.nn.sigmoid(logits), routes, axis=1)
    route_weights = chosen / jnp.sum(chosen, axis=1, keepdims=True) * route_scale
    expert_ids = routes.reshape(-1)
    onehot = (expert_ids[:, None] == jnp.arange(expert_count, dtype=jnp.int32)[None, :]).astype(
        jnp.int32
    )
    earlier = jnp.cumsum(onehot, axis=0) - onehot
    slot_index = jnp.sum(earlier * onehot, axis=1)
    slot_places = (expert_ids * slot_count + slot_index).reshape(token_count, top_count)
    slot_total = expert_count * slot_count
    placed = slot_places[None, :, :] == jnp.arange(slot_total, dtype=jnp.int32)[:, None, None]
    gather_matrix = jnp.any(placed, axis=2).astype(jnp.bfloat16)
    combine_matrix = jnp.sum(jnp.where(placed, route_weights[None, :, :], 0.0), axis=2).T
    outgoing = jnp.dot(gather_matrix, expert_in, preferred_element_type=jnp.float32).astype(
        jnp.bfloat16
    )
    outgoing = outgoing.reshape(owner_count, per_owner, slot_count, expert_in.shape[1])
    slab = lax.all_to_all(outgoing, "req", split_axis=0, concat_axis=0, tiled=True)
    gate_part = jnp.einsum("oesd,edf->oesf", slab, expert_gate, preferred_element_type=jnp.float32)
    up_part = jnp.einsum("oesd,edf->oesf", slab, expert_up, preferred_element_type=jnp.float32)
    inner_units = (jax.nn.silu(gate_part) * up_part).astype(jnp.bfloat16)
    partial_out = jnp.einsum(
        "oesf,efd->oesd", inner_units, expert_down, preferred_element_type=jnp.float32
    )
    results = lax.psum_scatter(partial_out, "tp", scatter_dimension=3, tiled=True)
    shared_inner = (
        jax.nn.silu(jnp.dot(expert_in, shared_gate, preferred_element_type=jnp.float32))
        * jnp.dot(expert_in, shared_up, preferred_element_type=jnp.float32)
    ).astype(jnp.bfloat16)
    shared_part = jnp.dot(shared_inner, shared_down, preferred_element_type=jnp.float32)
    returned = lax.all_to_all(results, "req", split_axis=0, concat_axis=0, tiled=True)
    routed = jnp.dot(
        combine_matrix, returned.reshape(slot_total, column_width), precision=lax.Precision.HIGHEST
    )
    shared_columns = lax.psum_scatter(shared_part, "tp", scatter_dimension=1, tiled=True)
    next_hidden = (mixed_columns.astype(jnp.float32) + routed + shared_columns).astype(jnp.bfloat16)
    return (next_hidden, new_rows)


def solution(mesh):
    in_specs = (
        P("req", "tp"),
        P("req"),
        P("req", None),
        P("req", None),
        P(),
        P(None, "tp"),
        P(None, "tp"),
        P(),
        P("tp", None, None),
        P("tp", None, None),
        P("tp", None),
        P(),
        P(),
        P("req", None, "tp"),
        P("req", None, "tp"),
        P("req", "tp", None),
        P(None, "tp"),
        P(None, "tp"),
        P("tp", None),
    )
    out_specs = (P("req", "tp"), P("req", None))
    return jax.shard_map(shards, mesh=mesh, in_specs=in_specs, out_specs=out_specs, check_vma=False)
```

profile of v0, /device:TPU:1, one launch (start us, length us, event | category | flops | bytes accessed | tf_op | source)
XLA Modules:
  0.0 509.0 jit_solution(7842593407011253523)
XLA Ops:
  7.2 16.5 %all_gather.6 = bf16[128,2048]{1,0:T(8,128)(2,1)S(1)} all-gather(bf16[128,256]{1,0:T(8,128)(2,1)} %param.19), channel_id=1, replica_groups=mesh['req'=32,'tp'=8] {'tp'}, dimensions={1}, use_global_device_ids=true | all-gather | bytes 589824 | tf_op jit(solution)/shard_map/all_gather | solution.py:94
  24.6 1.3 convolution_convert_fusion.2
  26.0 12.8 %all_gather.7 = bf16[128,576]{0,1:T(8,128)(2,1)S(1)} all-gather(bf16[128,72]{0,1:T(8,128)(2,1)S(1)} %convolution_convert_fusion.2), channel_id=1, replica_groups=mesh['req'=32,'tp'=8] {'tp'}, dimensions={1}, use_global_device_ids=true | all-gather | bytes 165888 | tf_op jit(solution)/shard_map/all_gather | solution.py:109
  40.5 0.8 copy.114
  41.7 0.7 copy.109
  42.4 0.7 copy.111
  43.1 0.8 fusion.70
  44.4 1.1 fusion.56
  45.5 0.9 subtract_convert_fusion
  46.6 2.9 select_reduce_fusion.1
  49.5 1.3 copy-done.2
  51.4 3.5 fusion.34
  55.0 1.4 fusion.95
  56.9 1.8 reduce-window.19
  59.3 1.1 fusion.4
  60.4 62.6 %all-reduce.2.cloned.1.call-done = f32[128,2048]{1,0:T(8,128)} async-done(((f32[128,2048]{1,0:T(8,128)}), f32[128,2048]{1,0:T(8,128)}) %all-reduce.2.cloned.1.call-update) | async-done | bytes 1048592 | tf_op jit(solution)/shard_map/psum | solution.py:123
  123.0 1.5 fusion.42
  124.4 2.4 convolution_convert_fusion
  126.9 190.3 %all_to_all.10 = bf16[32,2,32,2048]{3,2,1,0:T(8,128)(2,1)S(1)} all-to-all(bf16[32,2,32,2048]{3,2,1,0:T(8,128)(2,1)S(1)} %bitcast.104), channel_id=1, replica_groups=mesh['req'=32,'tp'=8] {'req'}, dimensions={0} | all-to-all | bytes 16777216 | tf_op jit(solution)/shard_map/all_to_all | solution.py:149
  317.2 3.2 copy-done.1
  320.4 3.7 fusion.2
  324.1 15.2 %convolution_bitcast_fusion = f32[32,2,32,2048]{3,2,0,1:T(8,128)} fusion(f32[2,32,32,176]{3,2,1,0:T(8,128)} %fusion.2, bf16[32,2,32,2048]{3,2,1,0:T(8,128)(2,1)} %copy-done.1, bf16[2,176,2048]{2,1,0:T(8,128)(2,1)} %param.34, bf16[2,2048,176]{1,2,0:T(8,128)(2,1)} %param.33), kind=kOutput, calls=%fused_computation.6 | convolution fusion | flops 2954952704 | bytes 29491200 | tf_op jit(solution)/shard_map/oesf,efd->oesd/dot_general | solution.py:153
  339.4 96.5 %reduce-scatter.3.cloned.1.call-done = f32[32,2,32,256]{3,2,0,1:T(8,128)} async-done(((f32[32,2,32,2048]{3,2,0,1:T(8,128)}), f32[32,2,32,256]{3,2,0,1:T(8,128)}) %reduce-scatter.3.cloned.1.call-update) | async-done | bytes 2097168 | tf_op jit(solution)/shard_map/reduce_scatter | solution.py:156
  435.8 3.2 copy.124
  439.0 9.8 %all-to-all-start.1 = ((f32[32,2,32,256]{3,2,1,0:T(8,128)}), f32[32,2,32,256]{3,2,1,0:T(8,128)}, u32[]{:S(2)}, u32[]{:S(2)}) async-start(f32[32,2,32,256]{3,2,1,0:T(8,128)} %copy.124), calls=%async_computation.2 | async-start | bytes 4194304 | tf_op jit(solution)/shard_map/all_to_all | solution.py:162
  448.9 1.5 fusion.88
  450.5 3.2 fusion.38
  454.3 5.1 %gather_fusion = f32[768]{0:T(1024)S(1)} fusion(f32[128,64]{0,1:T(8,128)S(1)} %fusion.41, s32[768]{0:T(1024)S(1)} %reshape.227), kind=kCustom, calls=%fused_computation | custom fusion | bytes 12288 | tf_op jit(solution)/shard_map/jit(take_along_axis)/gather | solution.py:132
  459.7 1.8 select_reduce_fusion
  461.5 25.5 %reduce-scatter.5.cloned.1.call-done = f32[128,256]{1,0:T(8,128)} async-done(((f32[128,2048]{1,0:T(8,128)}), f32[128,256]{1,0:T(8,128)}) %reduce-scatter.5.cloned.1.call-update) | async-done | bytes 131088 | tf_op jit(solution)/shard_map/reduce_scatter | solution.py:166
  487.0 11.1 %all-to-all-done.1 = f32[32,2,32,256]{3,2,1,0:T(8,128)} async-done(((f32[32,2,32,256]{3,2,1,0:T(8,128)}), f32[32,2,32,256]{3,2,1,0:T(8,128)}, u32[]{:S(2)}, u32[]{:S(2)}) %all-to-all-start.1) | async-done | bytes 2097184 | tf_op jit(solution)/shard_map/all_to_all | solution.py:162
  498.1 4.3 fusion.33
  (76 shorter events, 6.3 us)
Async XLA Ops:
  7.2 35.9 %copy-start = (bf16[2048,384]{1,0:T(8,128)(2,1)S(1)}, bf16[2048,384]{1,0:T(8,128)(2,1)}, u32[]{:S(2)}) copy-start(bf16[2048,384]{1,0:T(8,128)(2,1)} %param.24) | copy-start | bytes 4718596
  7.2 31.7 %copy-start.11 = (bf16[512]{0:T(512)(128)(2,1)S(1)}, bf16[512]{0:T(512)(128)(2,1)}, u32[]{:S(2)}) copy-start(bf16[512]{0:T(512)(128)(2,1)} %param.26) | copy-start | bytes 3076
  7.2 31.7 %copy-start.10 = (s32[128]{0:T(128)S(1)}, s32[128]{0:T(128)}, u32[]{:S(2)}) copy-start(s32[128]{0:T(128)} %param.20) | copy-start | bytes 1540
  7.2 115.8 %all-reduce.2.cloned.1.call-start = ((), (), s32[]{:S(2)}) async-start(), calls=%async_computation.4 | async-start | bytes 2097152 | tf_op jit(solution)/shard_map/psum | solution.py:123
  39.3 0.6 copy-start.8
  40.5 3.6 copy-start.6
  41.5 4.0 copy-start.5
  49.5 1.4 copy-start.2
  51.4 3.5 copy-start.3
  54.9 1.5 copy-start.7
  55.0 4.3 copy-start.9
  56.4 379.5 %reduce-scatter.3.cloned.1.call-start = ((), (), s32[]{:S(2)}) async-start(), calls=%async_computation.5 | async-start | bytes 18874368 | tf_op jit(solution)/shard_map/reduce_scatter | solution.py:156
  126.9 193.5 %copy-start.12 = (bf16[2,2048,176]{1,2,0:T(8,128)(2,1)S(1)}, bf16[2,2048,176]{1,2,0:T(8,128)(2,1)}, u32[]{:S(2)}) copy-start(bf16[2,2048,176]{1,2,0:T(8,128)(2,1)} %param.32) | copy-start | bytes 4325380
  317.2 3.2 copy-start.1
  439.0 11.4 %copy-start.4 = (bf16[176,2048]{1,0:T(8,128)(2,1)S(1)}, bf16[176,2048]{1,0:T(8,128)(2,1)}, u32[]{:S(2)}) copy-start(bf16[176,2048]{1,0:T(8,128)(2,1)} %param.37) | copy-start | bytes 2162692
  439.0 59.1 %all-to-all-start.1 = ((f32[32,2,32,256]{3,2,1,0:T(8,128)}), f32[32,2,32,256]{3,2,1,0:T(8,128)}, u32[]{:S(2)}, u32[]{:S(2)}) async-start(f32[32,2,32,256]{3,2,1,0:T(8,128)} %copy.124), calls=%async_computation.2 | async-start | bytes 4194304 | tf_op jit(solution)/shard_map/all_to_all | solution.py:162
  448.9 38.1 %reduce-scatter.5.cloned.1.call-start = ((), (), s32[]{:S(2)}) async-start(), calls=%async_computation.6 | async-start | bytes 1179648 | tf_op jit(solution)/shard_map/reduce_scatter | solution.py:166
  450.5 3.5 copy-start.13
Sparse Core Ops, SparseCore 0:
  56.5 66.4 all-reduce.1
  339.5 96.3 reduce-scatter.2
  453.8 33.1 reduce-scatter.4
where the time goes:
time: 510 us; the launch traced here: 509 us
  blocking collectives  220 us (43%)
  waiting for transfers between devices  196 us (38%)
  matrix products  40.9 us (8%)
  local copies, waits for them, and re-layouts  17.5 us (3%)
  between operations  14.1 us (3%)
  other arithmetic  11.2 us (2%)
  starting transfers between devices  9.94 us (2%)
    all_to_all x1, blocking collectives, shards(): lax.all_to_all(outgoing, 'req', split_axis=0, concat_axis=0, tiled=True)  190 us
    reduce_scatter x1, waiting for transfers between devices, shards(): lax.psum_scatter(partial_out, 'tp', scatter_dimension=3, tiled=True)  96.5 us
    psum x1, waiting for transfers between devices, shards(): total_attention = lax.psum(attention, 'tp')  62.6 us
    reduce_scatter x1, waiting for transfers between devices, shards(): lax.psum_scatter(shared_part, 'tp', scatter_dimension=1, tiled=True)  25.5 us
    all_gather x1, blocking collectives, shards(): whole = lax.all_gather(hidden, 'tp', axis=1, tiled=True)  16.5 us
    dot_general x1, matrix products, shards(): jnp.einsum('oesf,efd->oesd', inner_units, expert_down, preferred_element_...  15.2 us
    all_gather x1, blocking collectives, shards(): latent_raw = lax.all_gather(latent_part, 'tp', axis=1, tiled=True)  12.8 us
    all_to_all x1, waiting for transfers between devices, shards(): lax.all_to_all(results, 'req', split_axis=0, concat_axis=0, tiled=True)  11.1 us
  transfers between devices with their start and end apart: 4, of which 4 were waited for; matrix products, arithmetic and copies ran while one was open for 3% of the time, Pallas kernels for 0%

commit v1 on v0

--- a/solution.py
+++ b/solution.py
@@ -120,7 +120,11 @@
     attention = jnp.dot(
         head_values.reshape(token_count, -1), output_weight, preferred_element_type=jnp.float32
     )
-    total_attention = lax.psum(attention, "tp")
+    total_attention = attention
+    for hop in (1, 2, 4):
+        total_attention = total_attention + lax.ppermute(
+            total_attention, "tp", [(dev, dev ^ hop) for dev in range(8)]
+        )
     mixed = (whole.astype(jnp.float32) + total_attention).astype(jnp.bfloat16)
     mixed_columns = lax.dynamic_slice_in_dim(mixed, column_start, column_width, 1)
     expert_in = rms_norm(mixed, feedforward_gain).astype(jnp.bfloat16)

time: 510 us -> 496 us (0.973)
  waiting for transfers between devices: 196 us -> 181 us
    psum x1 -> x0, waiting for transfers between devices: 62.6 us -> none  [shards(): total_attention = lax.psum(attention, 'tp')]
    ppermute x0 -> x3, waiting for transfers between devices: none -> 47.1 us  [shards(): lax.ppermute(total_attention, 'tp', [(dev, dev ^ hop) for dev in range(8)])]
    all_to_all x1, waiting for transfers between devices: 11.1 us -> 38.8 us  [shards(): lax.all_to_all(results, 'req', split_axis=0, concat_axis=0, tiled=True)]
    reduce_scatter x1, waiting for transfers between devices: 25.5 us -> 0.02 us  [shards(): lax.psum_scatter(shared_part, 'tp', scatter_dimension=1, tiled=True)]
  transfers between devices with their start and end apart: 4 -> 6, of which waited for: 4 -> 5; matrix products, arithmetic and copies ran while one was open for 3% -> 4% of each run, Pallas kernels for 0% -> 0%
where the time goes in v1:
time: 496 us; the launch traced here: 495 us
  blocking collectives  221 us (45%)
  waiting for transfers between devices  181 us (36%)
  matrix products  37.1 us (7%)
  local copies, waits for them, and re-layouts  16.8 us (3%)
  between operations  14.5 us (3%)
  other arithmetic  13.4 us (3%)
  starting transfers between devices  11.7 us (2%)
    all_to_all x1, blocking collectives, shards(): lax.all_to_all(outgoing, 'req', split_axis=0, concat_axis=0, tiled=True)  191 us
    reduce_scatter x1, waiting for transfers between devices, shards(): lax.psum_scatter(partial_out, 'tp', scatter_dimension=3, tiled=True)  94.8 us
    ppermute x3, waiting for transfers between devices, shards(): lax.ppermute(total_attention, 'tp', [(dev, dev ^ hop) for dev in range(8)])  47.1 us
    all_to_all x1, waiting for transfers between devices, shards(): lax.all_to_all(results, 'req', split_axis=0, concat_axis=0, tiled=True)  38.8 us
    all_gather x1, blocking collectives, shards(): whole = lax.all_gather(hidden, 'tp', axis=1, tiled=True)  16.5 us
    dot_general x1, matrix products, shards(): jnp.einsum('oesf,efd->oesd', inner_units, expert_down, preferred_element_...  15.2 us
    all_gather x1, blocking collectives, shards(): latent_raw = lax.all_gather(latent_part, 'tp', axis=1, tiled=True)  12.8 us
  transfers between devices with their start and end apart: 6, of which 5 were waited for; matrix products, arithmetic and copies ran while one was open for 4% of the time, Pallas kernels for 0%

profile of v1, /device:TPU:1, one launch (start us, length us, event | category | flops | bytes accessed | tf_op | source)
XLA Modules:
  0.0 495.1 jit_solution(10745163291549391996)
XLA Ops:
  7.2 16.5 %all_gather.6 = bf16[128,2048]{1,0:T(8,128)(2,1)S(1)} all-gather(bf16[128,256]{1,0:T(8,128)(2,1)} %param.19), channel_id=1, replica_groups=mesh['req'=32,'tp'=8] {'tp'}, dimensions={1}, use_global_device_ids=true | all-gather | bytes 589824 | tf_op jit(solution)/shard_map/all_gather | solution.py:94
  24.6 1.3 convolution_convert_fusion.2
  26.0 12.8 %all_gather.7 = bf16[128,576]{0,1:T(8,128)(2,1)S(1)} all-gather(bf16[128,72]{0,1:T(8,128)(2,1)S(1)} %convolution_convert_fusion.2), channel_id=1, replica_groups=mesh['req'=32,'tp'=8] {'tp'}, dimensions={1}, use_global_device_ids=true | all-gather | bytes 165888 | tf_op jit(solution)/shard_map/all_gather | solution.py:109
  40.9 0.7 copy.109
  41.7 0.7 copy.111
  42.4 0.8 fusion.68
  43.7 1.1 fusion.54
  44.8 0.9 subtract_convert_fusion
  45.9 2.9 select_reduce_fusion.1
  48.8 1.3 copy-done.4
  50.7 3.4 fusion.32
  54.8 2.5 collective-permute-done
  57.5 24.5 %collective-permute-done.1 = f32[128,2048]{1,0:T(8,128)S(1)} collective-permute-done((f32[128,2048]{1,0:T(8,128)S(1)}, f32[128,2048]{1,0:T(8,128)S(1)}, u32[]{:S(2)}, u32[]{:S(2)}) %collective-permute-start.1) | collective-permute-done | bytes 1048608 | tf_op jit(solution)/shard_map/ppermute | solution.py:125
  82.2 1.5 collective-permute-start.2
  84.0 1.8 reduce-window.19
  86.5 1.1 fusion.4
  87.6 20.1 %collective-permute-done.2 = f32[128,2048]{1,0:T(8,128)} collective-permute-done((f32[128,2048]{1,0:T(8,128)S(1)}, f32[128,2048]{1,0:T(8,128)}, u32[]{:S(2)}, u32[]{:S(2)}) %collective-permute-start.2) | collective-permute-done | bytes 1048608 | tf_op jit(solution)/shard_map/ppermute | solution.py:125
  107.7 1.8 fusion.40
  109.6 2.4 convolution_convert_fusion
  112.0 191.5 %all_to_all.10 = bf16[32,2,32,2048]{3,2,1,0:T(8,128)(2,1)S(1)} all-to-all(bf16[32,2,32,2048]{3,2,1,0:T(8,128)(2,1)S(1)} %bitcast.104), channel_id=1, replica_groups=mesh['req'=32,'tp'=8] {'req'}, dimensions={0} | all-to-all | bytes 16777216 | tf_op jit(solution)/shard_map/all_to_all | solution.py:153
  303.5 3.2 copy-done.2
  306.7 3.8 fusion.2
  310.6 15.2 %convolution_bitcast_fusion = f32[32,2,32,2048]{3,2,0,1:T(8,128)} fusion(f32[2,32,32,176]{3,2,1,0:T(8,128)} %fusion.2, bf16[32,2,32,2048]{3,2,1,0:T(8,128)(2,1)} %copy-done.2, bf16[2,176,2048]{2,1,0:T(8,128)(2,1)} %param.34, bf16[2,2048,176]{1,2,0:T(8,128)(2,1)} %param.33), kind=kOutput, calls=%fused_computation.6 | convolution fusion | flops 2954952704 | bytes 29491200 | tf_op jit(solution)/shard_map/oesf,efd->oesd/dot_general | solution.py:157
  325.8 94.8 %reduce-scatter.3.cloned.1.call-done = f32[32,2,32,256]{3,2,0,1:T(8,128)} async-done(((f32[32,2,32,2048]{3,2,0,1:T(8,128)}), f32[32,2,32,256]{3,2,0,1:T(8,128)}) %reduce-scatter.3.cloned.1.call-update) | async-done | bytes 2097168 | tf_op jit(solution)/shard_map/reduce_scatter | solution.py:160
  420.6 3.2 copy.124
  423.8 9.8 %all-to-all-start.1 = ((f32[32,2,32,256]{3,2,1,0:T(8,128)}), f32[32,2,32,256]{3,2,1,0:T(8,128)}, u32[]{:S(2)}, u32[]{:S(2)}) async-start(f32[32,2,32,256]{3,2,1,0:T(8,128)} %copy.124), calls=%async_computation.2 | async-start | bytes 4194304 | tf_op jit(solution)/shard_map/all_to_all | solution.py:166
  434.1 2.0 fusion.36
  436.8 5.1 %gather_fusion = f32[768]{0:T(1024)S(1)} fusion(f32[128,64]{0,1:T(8,128)S(1)} %fusion.39, s32[768]{0:T(1024)S(1)} %reshape.227), kind=kCustom, calls=%fused_computation | custom fusion | bytes 12288 | tf_op jit(solution)/shard_map/jit(take_along_axis)/gather | solution.py:136
  442.2 1.8 select_reduce_fusion
  444.0 38.8 %all-to-all-done.1 = f32[32,2,32,256]{3,2,1,0:T(8,128)} async-done(((f32[32,2,32,256]{3,2,1,0:T(8,128)}), f32[32,2,32,256]{3,2,1,0:T(8,128)}, u32[]{:S(2)}, u32[]{:S(2)}) %all-to-all-start.1) | async-done | bytes 2097184 | tf_op jit(solution)/shard_map/all_to_all | solution.py:166
  482.8 3.8 fusion.94
  486.6 1.6 add_convert_fusion
  (92 shorter events, 7.7 us)
Async XLA Ops:
  7.2 35.2 %copy-start = (bf16[2048,384]{1,0:T(8,128)(2,1)S(1)}, bf16[2048,384]{1,0:T(8,128)(2,1)}, u32[]{:S(2)}) copy-start(bf16[2048,384]{1,0:T(8,128)(2,1)} %param.24) | copy-start | bytes 4718596
  7.2 31.7 %copy-start.14 = (bf16[512]{0:T(512)(128)(2,1)S(1)}, bf16[512]{0:T(512)(128)(2,1)}, u32[]{:S(2)}) copy-start(bf16[512]{0:T(512)(128)(2,1)} %param.26) | copy-start | bytes 3076
  7.2 31.7 %copy-start.13 = (s32[128]{0:T(128)S(1)}, s32[128]{0:T(128)}, u32[]{:S(2)}) copy-start(s32[128]{0:T(128)} %param.20) | copy-start | bytes 1540
  7.2 413.4 %reduce-scatter.3.cloned.1.call-start = ((), (), s32[]{:S(2)}) async-start(), calls=%async_computation.4 | async-start | bytes 18874368 | tf_op jit(solution)/shard_map/reduce_scatter | solution.py:160
  39.3 0.6 copy-start.11
  40.5 2.9 copy-start.9
  40.8 4.0 copy-start.8
  48.8 1.4 copy-start.4
  48.8 1.9 copy-start.17
  50.7 3.5 copy-start.5
  54.5 2.7 collective-permute-start
  57.4 26.2 %copy-start.10 = (s32[128,6]{0,1:T(8,128)S(1)}, s32[128,6]{0,1:T(8,128)}, u32[]{:S(2)}) copy-start(s32[128,6]{0,1:T(8,128)} %param.21) | copy-start | bytes 9220
  57.4 29.1 %copy-start.12 = (bf16[2048]{0:T(1024)(128)(2,1)S(1)}, bf16[2048]{0:T(1024)(128)(2,1)}, u32[]{:S(2)}) copy-start(bf16[2048]{0:T(1024)(128)(2,1)} %param.30) | copy-start | bytes 12292
  57.4 24.6 %collective-permute-start.1 = (f32[128,2048]{1,0:T(8,128)S(1)}, f32[128,2048]{1,0:T(8,128)S(1)}, u32[]{:S(2)}, u32[]{:S(2)}) collective-permute-start(f32[128,2048]{1,0:T(8,128)S(1)} %add.92), channel_id=1, source_target_pairs={{0,2},{1,3},{2,0},{3,1},{4,6},{5,7},{6,4},{7,5},{8,10},{9,11},{10,... | collective-permute-start | bytes 3145736 | tf_op jit(solution)/shard_map/ppermute | solution.py:125
  82.2 5.5 %copy-start.3 = (f32[128,2048]{1,0:T(8,128)}, f32[128,2048]{1,0:T(8,128)S(1)}, u32[]{:S(2)}) copy-start(f32[128,2048]{1,0:T(8,128)S(1)} %add.93) | copy-start | bytes 3145732
  82.2 25.6 %collective-permute-start.2 = (f32[128,2048]{1,0:T(8,128)S(1)}, f32[128,2048]{1,0:T(8,128)}, u32[]{:S(2)}, u32[]{:S(2)}) collective-permute-start(f32[128,2048]{1,0:T(8,128)S(1)} %add.93), channel_id=1, source_target_pairs={{0,4},{1,5},{2,6},{3,7},{4,0},{5,1},{6,2},{7,3},{8,12},{9,13},{10,... | collective-permute-start | bytes 3145736 | tf_op jit(solution)/shard_map/ppermute | solution.py:125
  112.0 194.7 %copy-start.15 = (bf16[2,2048,176]{1,2,0:T(8,128)(2,1)S(1)}, bf16[2,2048,176]{1,2,0:T(8,128)(2,1)}, u32[]{:S(2)}) copy-start(bf16[2,2048,176]{1,2,0:T(8,128)(2,1)} %param.32) | copy-start | bytes 4325380
  303.5 3.2 copy-start.2
  423.8 9.9 %copy-start.16 = (bf16[2048,176]{0,1:T(8,128)(2,1)S(1)}, bf16[2048,176]{0,1:T(8,128)(2,1)}, u32[]{:S(2)}) copy-start(bf16[2048,176]{0,1:T(8,128)(2,1)} %param.35) | copy-start | bytes 2162692
  423.8 10.3 %copy-start.6 = (bf16[176,2048]{1,0:T(8,128)(2,1)S(1)}, bf16[176,2048]{1,0:T(8,128)(2,1)}, u32[]{:S(2)}) copy-start(bf16[176,2048]{1,0:T(8,128)(2,1)} %param.37) | copy-start | bytes 2162692
  423.8 10.3 %copy-start.7 = (bf16[2048,176]{0,1:T(8,128)(2,1)S(1)}, bf16[2048,176]{0,1:T(8,128)(2,1)}, u32[]{:S(2)}) copy-start(bf16[2048,176]{0,1:T(8,128)(2,1)} %param.36) | copy-start | bytes 2162692
  423.8 59.1 %all-to-all-start.1 = ((f32[32,2,32,256]{3,2,1,0:T(8,128)}), f32[32,2,32,256]{3,2,1,0:T(8,128)}, u32[]{:S(2)}, u32[]{:S(2)}) async-start(f32[32,2,32,256]{3,2,1,0:T(8,128)} %copy.124), calls=%async_computation.2 | async-start | bytes 4194304 | tf_op jit(solution)/shard_map/all_to_all | solution.py:166
  433.6 53.1 %reduce-scatter.5.cloned.1.call-start = ((), (), s32[]{:S(2)}) async-start(), calls=%async_computation.5 | async-start | bytes 1179648 | tf_op jit(solution)/shard_map/reduce_scatter | solution.py:170
  434.1 2.3 copy-start.18
  442.2 46.0 %copy-start.1 = (bf16[2048,384]{1,0:T(8,128)(2,1)S(1)}, bf16[2048,384]{1,0:T(8,128)(2,1)}, u32[]{:S(2)}) copy-start(bf16[2048,384]{1,0:T(8,128)(2,1)} %param.24) | copy-start | bytes 4718596
Sparse Core Ops, SparseCore 0:
  325.9 94.6 reduce-scatter.2
  436.9 33.1 reduce-scatter.4
